TPU v7x, 128 devices: a whole 4x4x4 slice. The times are simulated.
128 devices in a mesh: img: 8 (over y, core), fsdp: 16 (over x, z).
Axes of the slice: x: 4, y: 4, z: 4, core: 2. Of those that a mesh axis runs over, the one named last changes fastest.
Arguments:
- text_states: bfloat16 [4096, 8192], P('img', 'fsdp'), may hold values from -100 to 100, as said below
- text_gain: float32 [8192], P('fsdp'), may hold values from 0.1 to 1.9
- gate_scale: float32 [8192], P('fsdp'), may hold values from 0.3 to 1.5
- live_counts: int32 [8], P('img'), may hold values from 1 to 512, 3072 in all
- token_slot: int32 [8, 512], P('img'), may hold values from 0 to 7, never falling along the last dimension, each value on 1 to 256 neighbouring positions
- wanted_images: int32 [8, 8], replicated, may hold values from 0 to 31, as said below
- patches: bfloat16 [32, 256, 1280], P('img', None, 'fsdp'), may hold values from -100 to 100, as said below
- latent_init: bfloat16 [64, 1280], replicated, may hold values from -100 to 100, as said below
- context_gain: float32 [1280], replicated, may hold values from 0.1 to 1.9
- latent_gain: float32 [1280], replicated, may hold values from 0.1 to 1.9
- res_query: bfloat16 [1280, 1536], P(None, 'fsdp'), may hold values from -0.15625 to 0.15625
- res_key: bfloat16 [1280, 1536], P(None, 'fsdp'), may hold values from -0.15625 to 0.15625
- res_value: bfloat16 [1280, 1536], P(None, 'fsdp'), may hold values from -0.15625 to 0.15625
- res_out: bfloat16 [1536, 1280], P('fsdp'), may hold values from -0.21875 to 0.21875
- final_gain: float32 [1280], P('fsdp'), may hold values from 0.1 to 1.9
- cross_query: bfloat16 [8192, 8192], P('fsdp'), may hold values from -0.09375 to 0.09375
- cross_key: bfloat16 [1280, 8192], P('fsdp'), may hold values from -0.25 to 0.25
- cross_value: bfloat16 [1280, 8192], P('fsdp'), may hold values from -0.25 to 0.25
- cross_out: bfloat16 [8192, 8192], P('fsdp'), may hold values from -0.09375 to 0.09375
Outputs:
- layer_output: float32 [4096, 8192], P('img', 'fsdp')
Inputs may be any that keep to these rules, and one draw needn't show every extreme that they name: `wanted_images`: image i is held by owner i // 4 along img. A row lists 8 distinct images; every owner that appears in a row has exactly 2 of its images there. `token_slot`: along a shard's tokens the slot never falls, and every slot of the shard is used. Tokens of shard s at positions live_counts[s] and beyond are padding. `text_states`: real values. `patches`: real values. `latent_init`: real values.
All inputs are finite; a program needn't handle non-finite values.
Results may differ from a plain program's by a relative error of at most 0.0075.
Values may be sent and summed in bfloat16 or wider, within the bound.
No kernel may reach another device: no remote copies, remote signals or barrier semaphores. Data moves between devices by JAX's collectives and lax.ppermute only.
A program may use at most 128 MiB of HBM per device.

v0:
```python
import jax
import jax.numpy as jnp
from jax import lax
from jax.sharding import PartitionSpec as P

D = 8192
HEAD = 128
RHD = 96
PAIR = 2
eps_norm = 1e-05
eps_rms = 1e-06


def layer_norm(values, gain_vec):
    values = values.astype(jnp.float32)
    row_mean = jnp.mean(values, -1, keepdims=True)
    spread = jnp.mean(values * values, -1, keepdims=True) - row_mean * row_mean
    return (values - row_mean) * lax.rsqrt(spread + eps_norm) * gain_vec


def route_tables(wanted_images, per_owner, pair_slots):
    owners = wanted_images // per_owner
    slot_total = wanted_images.shape[1]
    positions = jnp.arange(slot_total, dtype=jnp.int32)
    before = (owners[:, :, None] == owners[:, None, :]) & (
        positions[None, None, :] < positions[None, :, None]
    )
    slot_rank = jnp.sum(before.astype(jnp.int32), axis=2)
    rank_hot = (
        slot_rank[:, :, None] == jnp.arange(pair_slots, dtype=jnp.int32)[None, None, :]
    ).astype(jnp.float32)
    return (owners, rank_hot)


def pack_rows(row_data, wanted_images, my_shard, per_owner, pair_slots):
    owners, rank_hot = route_tables(wanted_images, per_owner, pair_slots)
    is_mine = (owners == my_shard).astype(jnp.float32)
    local_hot = (
        (wanted_images % per_owner)[:, :, None]
        == jnp.arange(per_owner, dtype=jnp.int32)[None, None, :]
    ).astype(jnp.float32)
    picker = jnp.einsum("scp,sci->spi", rank_hot * is_mine[:, :, None], local_hot).astype(
        jnp.bfloat16
    )
    return jnp.einsum("spi,if->spf", picker, row_data, preferred_element_type=jnp.float32).astype(
        jnp.bfloat16
    )


def unpack_rows(received, wanted_images, my_shard, per_owner, pair_slots):
    owners, rank_hot = route_tables(wanted_images, per_owner, pair_slots)
    owner_row = lax.dynamic_slice_in_dim(owners, my_shard, 1, 0)[0]
    rank_row = lax.dynamic_slice_in_dim(rank_hot, my_shard, 1, 0)[0]
    source_hot = (
        owner_row[:, None] == jnp.arange(received.shape[0], dtype=jnp.int32)[None, :]
    ).astype(jnp.float32)
    taker = (source_hot[:, :, None] * rank_row[:, None, :]).astype(jnp.bfloat16)
    return jnp.einsum("cop,opf->cf", taker, received, preferred_element_type=jnp.float32).astype(
        jnp.bfloat16
    )


def keyval_partial(flat_rows, cross_key, cross_value, head_cols, row_count):
    contract_first = (((0,), (1,)), ((), ()))
    block_count = row_count // (2 * head_cols)
    key_cols = lax.dot_general(
        cross_key, flat_rows, contract_first, preferred_element_type=jnp.float32
    )
    value_cols = lax.dot_general(
        cross_value, flat_rows, contract_first, preferred_element_type=jnp.float32
    )
    key_cols = key_cols.reshape(block_count, head_cols, flat_rows.shape[0])
    value_cols = value_cols.reshape(block_count, head_cols, flat_rows.shape[0])
    return jnp.concatenate([key_cols, value_cols], 1).reshape(row_count, flat_rows.shape[0])


def local(
    text_states,
    text_gain,
    gate_scale,
    live_counts,
    token_slot,
    wanted_images,
    patches,
    latent_init,
    context_gain,
    latent_gain,
    res_query,
    res_key,
    res_value,
    res_out,
    final_gain,
    cross_query,
    cross_key,
    cross_value,
    cross_out,
):
    my_feature = lax.axis_index("fsdp")
    my_shard = lax.axis_index("img")
    image_count = patches.shape[0]
    patch_count = patches.shape[1]
    feat_vis = patches.shape[2]
    latent_count = latent_init.shape[0]
    vis_width = latent_init.shape[1]
    res_cols = res_query.shape[1]
    res_heads = res_cols // RHD
    head_cols = cross_out.shape[0]
    token_count = text_states.shape[0]
    slot_count = wanted_images.shape[1]
    cross_heads = head_cols // HEAD
    contract_first = (((0,), (1,)), ((), ()))
    full_patches = lax.all_gather(patches, "fsdp", axis=2, tiled=True)
    context = layer_norm(full_patches, context_gain).astype(jnp.bfloat16)
    latent_normed = layer_norm(latent_init, latent_gain).astype(jnp.bfloat16)
    res_q_rows = jnp.dot(latent_normed, res_query, preferred_element_type=jnp.float32).astype(
        jnp.bfloat16
    )
    res_q_rows = res_q_rows.reshape(latent_count, res_heads, RHD)
    ctx_keys = jnp.einsum(
        "npv,vk->npk", context, res_key, preferred_element_type=jnp.float32
    ).astype(jnp.bfloat16)
    ctx_values = jnp.einsum(
        "npv,vk->npk", context, res_value, preferred_element_type=jnp.float32
    ).astype(jnp.bfloat16)
    lat_keys = jnp.dot(latent_normed, res_key, preferred_element_type=jnp.float32).astype(
        jnp.bfloat16
    )
    lat_values = jnp.dot(latent_normed, res_value, preferred_element_type=jnp.float32).astype(
        jnp.bfloat16
    )
    joined_shape = (image_count, latent_count, res_cols)
    key_rows = jnp.concatenate([ctx_keys, jnp.broadcast_to(lat_keys[None], joined_shape)], 1)
    value_rows = jnp.concatenate([ctx_values, jnp.broadcast_to(lat_values[None], joined_shape)], 1)
    key_rows = key_rows.reshape(image_count, patch_count + latent_count, res_heads, RHD)
    value_rows = value_rows.reshape(image_count, patch_count + latent_count, res_heads, RHD)
    res_scores = jnp.einsum(
        "rhe,nkhe->nhrk", res_q_rows, key_rows, preferred_element_type=jnp.float32
    ) * RHD ** (-0.5)
    res_weights = jnp.exp(res_scores)
    res_weights = (res_weights / jnp.sum(res_weights, -1, keepdims=True)).astype(jnp.bfloat16)
    res_mixed = jnp.einsum(
        "nhrk,nkhe->nrhe", res_weights, value_rows, preferred_element_type=jnp.float32
    )
    res_mixed = res_mixed.astype(jnp.bfloat16).reshape(image_count * latent_count, res_cols)
    columns = res_out
    mixed_sum = lax.psum_scatter(
        lax.dot_general(
            columns, res_mixed, contract_first, preferred_element_type=jnp.float32
        ).astype(jnp.bfloat16),
        "fsdp",
        scatter_dimension=0,
        tiled=True,
    ).astype(jnp.float32)
    init_cols = lax.dynamic_slice_in_dim(latent_init, my_feature * feat_vis, feat_vis, 1).astype(
        jnp.float32
    )
    latents = init_cols[None] + jnp.transpose(mixed_sum).reshape(
        image_count, latent_count, feat_vis
    )
    sum_first, sum_second = lax.psum((jnp.sum(latents, -1), jnp.sum(latents * latents, -1)), "fsdp")
    row_mean = sum_first / vis_width
    spread = sum_second / vis_width - row_mean * row_mean
    resampled = (
        (latents - row_mean[..., None]) * lax.rsqrt(spread + eps_norm)[..., None] * final_gain
    ).astype(jnp.bfloat16)
    text_f = text_states.astype(jnp.float32)
    squares = lax.psum(jnp.sum(text_f * text_f, -1), "fsdp")
    normed = (text_f * lax.rsqrt(squares / D + eps_rms)[:, None] * text_gain).astype(jnp.bfloat16)
    columns = cross_query
    query_cols = lax.psum_scatter(
        lax.dot_general(columns, normed, contract_first, preferred_element_type=jnp.float32).astype(
            jnp.bfloat16
        ),
        "fsdp",
        scatter_dimension=0,
        tiled=True,
    )
    per_image = resampled.reshape(image_count, latent_count * feat_vis)
    outgoing = pack_rows(per_image, wanted_images, my_shard, image_count, PAIR)
    incoming = lax.all_to_all(outgoing, "img", split_axis=0, concat_axis=0, tiled=True)
    slot_latents = unpack_rows(incoming, wanted_images, my_shard, image_count, PAIR).reshape(
        slot_count * latent_count, feat_vis
    )
    slot_kv = lax.psum_scatter(
        keyval_partial(
            slot_latents, cross_key, cross_value, head_cols, 2 * head_cols * lax.axis_size("fsdp")
        ).astype(jnp.bfloat16),
        "fsdp",
        scatter_dimension=0,
        tiled=True,
    )
    kv_slots = jnp.transpose(slot_kv.reshape(2 * head_cols, slot_count, latent_count), (1, 0, 2))
    query_heads = query_cols.reshape(cross_heads, HEAD, token_count)
    slot_keys = kv_slots[:, :head_cols].reshape(slot_count, cross_heads, HEAD, latent_count)
    slot_values = kv_slots[:, head_cols:].reshape(slot_count, cross_heads, HEAD, latent_count)
    scores = jnp.einsum(
        "het,cher->htcr", query_heads, slot_keys, preferred_element_type=jnp.float32
    ) * HEAD ** (-0.5)
    slot_hot = (token_slot[0][:, None] == jnp.arange(slot_count, dtype=jnp.int32)[None, :]).astype(
        jnp.float32
    )
    weights = jnp.exp(scores) * slot_hot[None, :, :, None]
    weights = (weights / jnp.sum(weights, axis=(2, 3), keepdims=True)).astype(jnp.bfloat16)
    attended = jnp.einsum(
        "htcr,cher->het", weights, slot_values, preferred_element_type=jnp.float32
    )
    attended = attended.astype(jnp.bfloat16).reshape(head_cols, token_count)
    columns = cross_out
    projected_cols = lax.psum_scatter(
        lax.dot_general(
            columns, attended, (((0,), (0,)), ((), ())), preferred_element_type=jnp.float32
        ).astype(jnp.bfloat16),
        "fsdp",
        scatter_dimension=0,
        tiled=True,
    ).astype(jnp.float32)
    projected = jnp.transpose(projected_cols)
    positions = jnp.arange(token_count, dtype=jnp.int32)
    live_mask = (positions < live_counts[0]).astype(jnp.float32)[:, None]
    return text_f + jnp.tanh(gate_scale) * projected * live_mask


def solution(mesh):
    placed = (
        P("img", "fsdp"),
        P("fsdp"),
        P("fsdp"),
        P("img"),
        P("img", None),
        P(),
        P("img", None, "fsdp"),
        P(),
        P(),
        P(),
        P(None, "fsdp"),
        P(None, "fsdp"),
        P(None, "fsdp"),
        P("fsdp", None),
        P("fsdp"),
        P("fsdp", None),
        P("fsdp", None),
        P("fsdp", None),
        P("fsdp", None),
    )
    return jax.shard_map(
        local, mesh=mesh, in_specs=placed, out_specs=P("img", "fsdp"), check_vma=False
    )
```

profile of v0, /device:TPU:0, one launch (start us, length us, event | category | flops | bytes accessed | tf_op | source)
XLA Modules:
  0.0 494.0 jit_solution(16812852713913608499)
XLA Ops:
  6.6 0.7 all-gather.2.cloned.1.call-update
  7.3 1.1 convert_reduce_fusion.1
  8.4 1.3 convolution_convert_fusion.10
  9.8 1.3 convolution_convert_fusion.11
  11.3 46.9 %all-gather.2.cloned.1.call-done = bf16[4,256,1280]{1,2,0:T(8,128)(2,1)} async-done(((bf16[4,256,80]{1,2,0:T(8,128)(2,1)}), bf16[4,256,1280]{1,2,0:T(8,128)(2,1)}) %all-gather.2.cloned.1.call-update) | async-done | bytes 2621456 | tf_op jit(solution)/shard_map/all_gather | solution.py:112
  58.2 2.4 convert_reduce_fusion
  60.6 2.8 convolution_convert_fusion.6
  64.2 2.8 convolution_convert_fusion.7
  67.7 1.1 copy.49
  69.1 72.8 %reduce-scatter.13.cloned.1.call-done = bf16[80,256]{1,0:T(8,128)(2,1)} async-done(((bf16[1280,256]{1,0:T(8,128)(2,1)}), bf16[80,256]{1,0:T(8,128)(2,1)}) %reduce-scatter.13.cloned.1.call-update) | async-done | bytes 40976
  141.9 0.9 copy.50
  143.1 38.6 %all-reduce = (f32[512]{0:T(512)S(1)}, f32[4,64]{1,0:T(4,128)S(1)}, f32[4,64]{1,0:T(4,128)S(1)}) all-reduce(f32[512]{0:T(512)S(1)} %fusion.15, f32[4,64]{1,0:T(4,128)S(1)} %reduce_sum.107, f32[4,64]{1,0:T(4,128)S(1)} %reduce_sum.105), channel_id=1, replica_groups=mesh['img'=8,'fsdp'=16] {'fsdp'}, use_global_device_ids=true, to_apply=%region_13.14 | all-reduce | flops 1024 | bytes 8192 | tf_op jit(solution)/shard_map/psum | solution.py:167
  181.7 10.2 %fusion = bf16[8192,512]{0,1:T(8,128)(2,1)} fusion(bf16[512,8192]{1,0:T(8,128)(2,1)} %param.34, bf16[512,512]{1,0:T(8,128)(2,1)S(1)} %copy-done.2, f32[512]{0:T(512)S(1)} %copy-done.14, f32[512]{0:T(512)S(1)} %add_rsqrt_fusion.1), kind=kOutput, calls=%fused_computation.5 | convolution fusion | flops 4300210176 | bytes 17305600 | tf_op jit(solution)/shard_map/dot_general | solution.py:171
  194.0 0.8 copy.39
  194.9 4.3 all-to-all-start
  199.5 6.2 %all-to-all-done = bf16[8,2,5120]{2,1,0:T(2,128)(2,1)S(1)} async-done(((bf16[8,2,5120]{2,1,0:T(2,128)(2,1)}), bf16[8,2,5120]{2,1,0:T(2,128)(2,1)S(1)}, u32[]{:S(2)}, u32[]{:S(2)}) %all-to-all-start) | async-done | bytes 163872 | tf_op jit(solution)/shard_map/all_to_all | solution.py:180
  206.1 5.6 %convolution_convert_fusion.3 = bf16[512,8192]{1,0:T(8,128)(2,1)} fusion(bf16[512,80]{1,0:T(8,128)(2,1)S(1)} %reshape.194, bf16[80,8192]{1,0:T(8,128)(2,1)S(1)} %copy-done), kind=kOutput, calls=%fused_computation.4 | convolution fusion | flops 675282944 | bytes 9781248 | tf_op jit(solution)/shard_map/dot_general | solution.py:66
  211.7 11.6 %copy.53 = bf16[64,8,16,512]{3,2,1,0:T(8,128)(2,1)} copy(bf16[64,8,16,512]{3,1,2,0:T(8,128)(2,1)} %bitcast.115) | data formatting | bytes 16777216
  223.2 5.5 %convolution_convert_fusion.2 = bf16[512,8192]{1,0:T(8,128)(2,1)} fusion(bf16[512,80]{1,0:T(8,128)(2,1)S(1)} %reshape.194, bf16[80,8192]{1,0:T(8,128)(2,1)S(1)} %copy-done.3), kind=kOutput, calls=%fused_computation.3 | convolution fusion | flops 675282944 | bytes 9781248 | tf_op jit(solution)/shard_map/dot_general | solution.py:69
  228.8 11.4 %copy.54 = bf16[64,8,16,512]{3,2,1,0:T(8,128)(2,1)} copy(bf16[64,8,16,512]{3,1,2,0:T(8,128)(2,1)} %bitcast.114) | data formatting | bytes 16777216
  240.2 8.4 %pad_maximum_fusion = bf16[16,1024,512]{1,0,2:T(8,128)(2,1)S(1)} fusion(bf16[16,512,512]{1,0,2:T(8,128)(2,1)} %bitcast.117, bf16[16,512,512]{1,0,2:T(8,128)(2,1)} %bitcast.116), kind=kLoop, calls=%fused_computation | loop fusion | flops 33554432 | bytes 33554432 | tf_op jit(solution)/shard_map/concatenate | solution.py:74
  248.6 12.0 %copy.55 = bf16[64,8,16,1024]{3,1,2,0:T(8,128)(2,1)} copy(bf16[64,8,16,1024]{3,2,1,0:T(8,128)(2,1)S(1)} %bitcast.113) | data formatting | bytes 33554432
  261.3 13.3 %reduce-scatter.9.cloned.1.call-done = bf16[512,512]{0,1:T(8,128)(2,1)} async-done(((bf16[8192,512]{0,1:T(8,128)(2,1)}), bf16[512,512]{0,1:T(8,128)(2,1)}) %reduce-scatter.9.cloned.1.call-update) | async-done | bytes 524304 | tf_op jit(solution)/shard_map/reduce_scatter | solution.py:170
  274.5 1.3 copy.48
  275.8 112.3 %reduce-scatter.7.cloned.1.call-done = bf16[1024,512]{0,1:T(8,128)(2,1)} async-done(((bf16[16384,512]{0,1:T(8,128)(2,1)}), bf16[1024,512]{0,1:T(8,128)(2,1)}) %reduce-scatter.7.cloned.1.call-update) | async-done | bytes 1048592 | tf_op jit(solution)/shard_map/reduce_scatter | solution.py:184
  388.1 1.3 slice_bitcast_fusion.1
  389.4 0.9 fusion.7
  390.3 1.0 fusion.11
  391.6 1.5 slice-done.1
  393.1 6.9 %fusion.1 = bf16[8192,512]{0,1:T(8,128)(2,1)} fusion(bf16[512,512]{1,0:T(8,128)(2,1)S(1)} %bitcast.122, bf16[512,8192]{1,0:T(8,128)(2,1)S(1)} %bitcast.119), kind=kOutput, calls=%fused_computation.6 | convolution fusion | flops 4299161600 | bytes 17301504 | tf_op jit(solution)/shard_map/dot_general | solution.py:210
  400.8 84.4 %reduce-scatter.11.cloned.1.call-done = bf16[512,512]{0,1:T(8,128)(2,1)} async-done(((bf16[8192,512]{0,1:T(8,128)(2,1)}), bf16[512,512]{0,1:T(8,128)(2,1)}) %reduce-scatter.11.cloned.1.call-update) | async-done | bytes 524304 | tf_op jit(solution)/shard_map/reduce_scatter | solution.py:209
  485.3 2.2 convert_add_fusion
  (83 shorter events, 6.0 us)
Async XLA Ops:
  6.5 199.6 %copy-start = (bf16[80,8192]{1,0:T(8,128)(2,1)S(1)}, bf16[80,8192]{1,0:T(8,128)(2,1)}, u32[]{:S(2)}) copy-start(bf16[80,8192]{1,0:T(8,128)(2,1)} %param.35) | copy-start | bytes 3932164
  6.5 56.9 %copy-start.5 = (bf16[64,1280]{1,0:T(8,128)(2,1)S(1)}, bf16[64,1280]{1,0:T(8,128)(2,1)}, u32[]{:S(2)}) copy-start(bf16[64,1280]{1,0:T(8,128)(2,1)} %param.26) | copy-start | bytes 491524
  6.5 56.9 %copy-start.12 = (f32[1280]{0:T(1024)S(1)}, f32[1280]{0:T(1024)}, u32[]{:S(2)}) copy-start(f32[1280]{0:T(1024)} %param.28) | copy-start | bytes 15364
  6.5 56.9 %copy-start.10 = (bf16[1280,96]{0,1:T(8,128)(2,1)S(1)}, bf16[1280,96]{0,1:T(8,128)(2,1)}, u32[]{:S(2)}) copy-start(bf16[1280,96]{0,1:T(8,128)(2,1)} %param.29) | copy-start | bytes 737284
  6.5 51.6 %all-gather.2.cloned.1.call-start = ((), (), s32[]{:S(2)}) async-start(), calls=%async_computation.5 | async-start | bytes 2785280 | tf_op jit(solution)/shard_map/all_gather | solution.py:112
  7.3 134.6 %reduce-scatter.13.cloned.1.call-start = ((), (), s32[]{:S(2)}) async-start(), calls=%async_computation.9 | async-start | bytes 696320
  9.8 54.3 %copy-start.11 = (bf16[1280,96]{0,1:T(8,128)(2,1)S(1)}, bf16[1280,96]{0,1:T(8,128)(2,1)}, u32[]{:S(2)}) copy-start(bf16[1280,96]{0,1:T(8,128)(2,1)} %param.31) | copy-start | bytes 737284
  9.8 54.3 %copy-start.13 = (f32[1280]{0:T(1024)S(1)}, f32[1280]{0:T(1024)}, u32[]{:S(2)}) copy-start(f32[1280]{0:T(1024)} %param.27) | copy-start | bytes 15364
  63.4 3.9 copy-start.4
  64.1 4.8 copy-start.2
  64.1 117.5 %copy-start.14 = (f32[512]{0:T(512)S(1)}, f32[512]{0:T(512)}, u32[]{:S(2)}) copy-start(f32[512]{0:T(512)} %param.20) | copy-start | bytes 6148
  68.8 205.8 %reduce-scatter.9.cloned.1.call-start = ((), (), s32[]{:S(2)}) async-start(), calls=%async_computation.7 | async-start | bytes 8912896 | tf_op jit(solution)/shard_map/reduce_scatter | solution.py:170
  191.9 0.7 copy-start.9
  191.9 0.7 copy-start.6
  194.9 10.7 %all-to-all-start = ((bf16[8,2,5120]{2,1,0:T(2,128)(2,1)}), bf16[8,2,5120]{2,1,0:T(2,128)(2,1)S(1)}, u32[]{:S(2)}, u32[]{:S(2)}) async-start(bf16[8,2,5120]{2,1,0:T(2,128)(2,1)} %copy.39), calls=%async_computation | async-start | bytes 327680 | tf_op jit(solution)/shard_map/all_to_all | solution.py:180
  199.2 188.9 %reduce-scatter.7.cloned.1.call-start = ((), (), s32[]{:S(2)}) async-start(), calls=%async_computation.6 | async-start | bytes 17825792 | tf_op jit(solution)/shard_map/reduce_scatter | solution.py:184
  211.7 11.6 %copy-start.3 = (bf16[80,8192]{1,0:T(8,128)(2,1)S(1)}, bf16[80,8192]{1,0:T(8,128)(2,1)}, u32[]{:S(2)}) copy-start(bf16[80,8192]{1,0:T(8,128)(2,1)} %param.36) | copy-start | bytes 3932164
  260.6 0.7 copy-start.7
  260.6 224.7 %reduce-scatter.11.cloned.1.call-start = ((), (), s32[]{:S(2)}) async-start(), calls=%async_computation.8 | async-start | bytes 8912896 | tf_op jit(solution)/shard_map/reduce_scatter | solution.py:209
  389.4 2.2 slice-start
  390.3 2.8 slice-start.1
  400.0 0.8 copy-start.8
  400.0 87.5 %copy-start.1 = (bf16[80,8192]{1,0:T(8,128)(2,1)S(1)}, bf16[80,8192]{1,0:T(8,128)(2,1)}, u32[]{:S(2)}) copy-start(bf16[80,8192]{1,0:T(8,128)(2,1)} %param.35) | copy-start | bytes 3932164
Sparse Core Ops, SparseCore 0:
  9.5 48.6 all-gather.1
  68.9 72.9 reduce-scatter.12
  192.1 82.4 reduce-scatter.8
  277.8 110.2 reduce-scatter.6
  400.2 85.0 reduce-scatter.10
where the time goes:
time: 495 us; the launch traced here: 494 us
  waiting for transfers between devices  337 us (68%)
  local copies, waits for them, and re-layouts  44.7 us (9%)
  matrix products  40.3 us (8%)
  blocking collectives  38.6 us (8%)
  other arithmetic  14.9 us (3%)
  between operations  14.3 us (3%)
    reduce_scatter x1, waiting for transfers between devices, local(): lax.psum_scatter(keyval_partial(slot_latents, cross_key, cross_value, hea...  112 us
    reduce_scatter x1, waiting for transfers between devices, local(): lax.psum_scatter(lax.dot_general(columns, attended, (((0,), (0,)), ((), (...  84.4 us
    unnamed x6, waiting for transfers between devices  73.5 us
    all_gather x1, waiting for transfers between devices, local(): full_patches = lax.all_gather(patches, 'fsdp', axis=2, tiled=True)  46.9 us
    unnamed x40, local copies, waits for them, and re-layouts  41.2 us
    psum x1, blocking collectives, local(): squares = lax.psum(jnp.sum(text_f * text_f, -1), 'fsdp')  38.6 us
    reduce_scatter x1, waiting for transfers between devices, local(): lax.psum_scatter(lax.dot_general(columns, normed, contract_first, preferr...  13.3 us
    dot_general x1, matrix products, local(): lax.dot_general(columns, normed, contract_first, preferred_element_type=j...  10.2 us
  transfers between devices with their start and end apart: 6, of which 6 were waited for; matrix products, arithmetic and copies ran while one was open for 13% of the time, Pallas kernels for 0%

commit v1 on v0

--- a/solution.py
+++ b/solution.py
@@ -9,6 +9,19 @@
 PAIR = 2
 eps_norm = 1e-05
 eps_rms = 1e-06
+
+
+def gather_around(x, axis, dim):
+    ways = lax.axis_size(axis)
+    up = [(d, (d + 1) % ways) for d in range(ways)]
+    down = [(d, (d - 1) % ways) for d in range(ways)]
+    earlier, later = ([x], [x])
+    for _ in range(ways // 2):
+        earlier.append(lax.ppermute(earlier[-1], axis, up))
+    for _ in range((ways - 1) // 2):
+        later.append(lax.ppermute(later[-1], axis, down))
+    line = jnp.concatenate([*earlier[::-1], *later[1:]], axis=dim)
+    return jnp.roll(line, (lax.axis_index(axis) - ways // 2) * x.shape[dim], axis=dim)
 
 
 def layer_norm(values, gain_vec):
@@ -109,7 +122,7 @@
     slot_count = wanted_images.shape[1]
     cross_heads = head_cols // HEAD
     contract_first = (((0,), (1,)), ((), ()))
-    full_patches = lax.all_gather(patches, "fsdp", axis=2, tiled=True)
+    full_patches = gather_around(patches, "fsdp", 2)
     context = layer_norm(full_patches, context_gain).astype(jnp.bfloat16)
     latent_normed = layer_norm(latent_init, latent_gain).astype(jnp.bfloat16)
     res_q_rows = jnp.dot(latent_normed, res_query, preferred_element_type=jnp.float32).astype(

time: 495 us -> 529 us (1.069); the launches traced: 494 us -> 520 us
  starting transfers between devices: 4.66 us -> 45.2 us
  waiting for transfers between devices: 337 us -> 318 us
    all_gather x1 -> x0, waiting for transfers between devices: 46.9 us -> none  [local(): full_patches = lax.all_gather(patches, 'fsdp', axis=2, tiled=True)]
    ppermute x0 -> x15, starting transfers between devices: none -> 40.8 us  [the longest x7 38.8 us: gather_around(): later.append(lax.ppermute(later[-1], axis, down))]
    ppermute x0 -> x15, waiting for transfers between devices: none -> 28.4 us  [the longest x8 27.7 us: gather_around(): earlier.append(lax.ppermute(earlier[-1], axis, up))]
    unnamed x40 -> x75, local copies, waits for them, and re-layouts: 41.2 us -> 46.2 us
    unnamed x6 -> x5, waiting for transfers between devices: 73.5 us -> 73.3 us
  transfers between devices with their start and end apart: 6 -> 20, of which waited for: 6 -> 14; matrix products, arithmetic and copies ran while one was open for 13% -> 13% of each run, Pallas kernels for 0% -> 0%
where the time goes in v1:
time: 529 us; the launch traced here: 520 us
  waiting for transfers between devices  318 us (60%)
  local copies, waits for them, and re-layouts  49.7 us (9%)
  starting transfers between devices  45.2 us (9%)
  matrix products  39.1 us (7%)
  blocking collectives  39 us (7%)
  between operations  14.8 us (3%)
  other arithmetic  13.6 us (3%)
    reduce_scatter x1, waiting for transfers between devices, local(): lax.psum_scatter(keyval_partial(slot_latents, cross_key, cross_value, hea...  112 us
    reduce_scatter x1, waiting for transfers between devices, local(): lax.psum_scatter(lax.dot_general(columns, attended, (((0,), (0,)), ((), (...  84.6 us
    unnamed x5, waiting for transfers between devices  73.3 us
    unnamed x75, local copies, waits for them, and re-layouts  46.2 us
    psum x1, blocking collectives, local(): squares = lax.psum(jnp.sum(text_f * text_f, -1), 'fsdp')  39 us
    ppermute x7, starting transfers between devices, gather_around(): later.append(lax.ppermute(later[-1], axis, down))  38.8 us
    ppermute x8, waiting for transfers between devices, gather_around(): earlier.append(lax.ppermute(earlier[-1], axis, up))  27.7 us
    reduce_scatter x1, waiting for transfers between devices, local(): lax.psum_scatter(lax.dot_general(columns, normed, contract_first, preferr...  13.1 us
  transfers between devices with their start and end apart: 20, of which 14 were waited for; matrix products, arithmetic and copies ran while one was open for 13% of the time, Pallas kernels for 0%

profile of v1, /device:TPU:0, one launch (start us, length us, event | category | flops | bytes accessed | tf_op | source)
XLA Modules:
  0.0 519.5 jit_solution(6277490290760624686)
XLA Ops:
  6.5 2.0 collective-permute-start
  8.6 8.8 %collective-permute-done = bf16[4,256,80]{1,2,0:T(8,128)(2,1)S(1)} collective-permute-done((bf16[4,256,80]{1,2,0:T(8,128)(2,1)}, bf16[4,256,80]{1,2,0:T(8,128)(2,1)S(1)}, u32[]{:S(2)}, u32[]{:S(2)}) %collective-permute-start) | collective-permute-done | bytes 163872 | tf_op jit(solution)/shard_map/ppermute | solution.py:20
  17.3 5.3 %collective-permute-start.8 = (bf16[4,256,80]{1,2,0:T(8,128)(2,1)}, bf16[4,256,80]{1,2,0:T(8,128)(2,1)S(1)}, u32[]{:S(2)}, u32[]{:S(2)}) collective-permute-start(bf16[4,256,80]{1,2,0:T(8,128)(2,1)} %param.25), channel_id=1, source_target_pairs={{0,15},{1,0},{2,1},{3,2},{4,3},{5,4},{6,5},{7,6},{8,7},{9,8},{10,9... | collective-permute-start | bytes 491528 | tf_op jit(solution)/shard_map/ppermute | solution.py:22
  22.7 3.3 collective-permute-done.1
  26.0 5.5 %collective-permute-start.9 = (bf16[4,256,80]{1,2,0:T(8,128)(2,1)S(1)}, bf16[4,256,80]{1,2,0:T(8,128)(2,1)S(1)}, u32[]{:S(2)}, u32[]{:S(2)}) collective-permute-start(bf16[4,256,80]{1,2,0:T(8,128)(2,1)S(1)} %collective-permute-done.8), channel_id=1, source_target_pairs={{0,15},{1,0},{2,1},{3,2},{4,3},{5,4},{6,5},{7,6},{8,7},{9,8},{10,9... | collective-permute-start | bytes 491528 | tf_op jit(solution)/shard_map/ppermute | solution.py:22
  31.5 3.1 collective-permute-done.2
  34.7 5.5 %collective-permute-start.10 = (bf16[4,256,80]{1,2,0:T(8,128)(2,1)S(1)}, bf16[4,256,80]{1,2,0:T(8,128)(2,1)S(1)}, u32[]{:S(2)}, u32[]{:S(2)}) collective-permute-start(bf16[4,256,80]{1,2,0:T(8,128)(2,1)S(1)} %collective-permute-done.9), channel_id=1, source_target_pairs={{0,15},{1,0},{2,1},{3,2},{4,3},{5,4},{6,5},{7,6},{8,7},{9,8},{10,9... | collective-permute-start | bytes 491528 | tf_op jit(solution)/shard_map/ppermute | solution.py:22
  40.2 3.1 collective-permute-done.3
  44.4 5.4 %collective-permute-start.11 = (bf16[4,256,80]{1,2,0:T(8,128)(2,1)S(1)}, bf16[4,256,80]{1,2,0:T(8,128)(2,1)S(1)}, u32[]{:S(2)}, u32[]{:S(2)}) collective-permute-start(bf16[4,256,80]{1,2,0:T(8,128)(2,1)S(1)} %collective-permute-done.10), channel_id=1, source_target_pairs={{0,15},{1,0},{2,1},{3,2},{4,3},{5,4},{6,5},{7,6},{8,7},{9,8},{10,9... | collective-permute-start | bytes 491528 | tf_op jit(solution)/shard_map/ppermute | solution.py:22
  49.8 2.2 collective-permute-done.4
  52.6 5.8 %collective-permute-start.12 = (bf16[4,256,80]{1,2,0:T(8,128)(2,1)S(1)}, bf16[4,256,80]{1,2,0:T(8,128)(2,1)S(1)}, u32[]{:S(2)}, u32[]{:S(2)}) collective-permute-start(bf16[4,256,80]{1,2,0:T(8,128)(2,1)S(1)} %collective-permute-done.11), channel_id=1, source_target_pairs={{0,15},{1,0},{2,1},{3,2},{4,3},{5,4},{6,5},{7,6},{8,7},{9,8},{10,9... | collective-permute-start | bytes 491528 | tf_op jit(solution)/shard_map/ppermute | solution.py:22
  58.4 2.4 collective-permute-done.5
  62.3 5.4 %collective-permute-start.13 = (bf16[4,256,80]{1,2,0:T(8,128)(2,1)S(1)}, bf16[4,256,80]{1,2,0:T(8,128)(2,1)S(1)}, u32[]{:S(2)}, u32[]{:S(2)}) collective-permute-start(bf16[4,256,80]{1,2,0:T(8,128)(2,1)S(1)} %collective-permute-done.12), channel_id=1, source_target_pairs={{0,15},{1,0},{2,1},{3,2},{4,3},{5,4},{6,5},{7,6},{8,7},{9,8},{10,9... | collective-permute-start | bytes 491528 | tf_op jit(solution)/shard_map/ppermute | solution.py:22
  67.7 3.0 collective-permute-done.6
  72.1 5.8 %collective-permute-start.14 = (bf16[4,256,80]{1,2,0:T(8,128)(2,1)S(1)}, bf16[4,256,80]{1,2,0:T(8,128)(2,1)S(1)}, u32[]{:S(2)}, u32[]{:S(2)}) collective-permute-start(bf16[4,256,80]{1,2,0:T(8,128)(2,1)S(1)} %collective-permute-done.13), channel_id=1, source_target_pairs={{0,15},{1,0},{2,1},{3,2},{4,3},{5,4},{6,5},{7,6},{8,7},{9,8},{10,9... | collective-permute-start | bytes 491528 | tf_op jit(solution)/shard_map/ppermute | solution.py:22
  87.6 2.1 convolution_convert_fusion.7
  93.4 73.2 %reduce-scatter.13.cloned.1.call-done = bf16[80,256]{1,0:T(8,128)(2,1)} async-done(((bf16[1280,256]{1,0:T(8,128)(2,1)}), bf16[80,256]{1,0:T(8,128)(2,1)}) %reduce-scatter.13.cloned.1.call-update) | async-done | bytes 40976
  167.8 39.0 %all-reduce = (f32[512]{0:T(512)S(1)}, f32[4,64]{1,0:T(4,128)S(1)}, f32[4,64]{1,0:T(4,128)S(1)}) all-reduce(f32[512]{0:T(512)S(1)} %fusion.15, f32[4,64]{1,0:T(4,128)S(1)} %reduce_sum.107, f32[4,64]{1,0:T(4,128)S(1)} %reduce_sum.105), channel_id=1, replica_groups=mesh['img'=8,'fsdp'=16] {'fsdp'}, use_global_device_ids=true, to_apply=%region_13.14 | all-reduce | flops 1024 | bytes 8192 | tf_op jit(solution)/shard_map/psum | solution.py:180
  206.8 10.3 %fusion = bf16[8192,512]{0,1:T(8,128)(2,1)} fusion(bf16[512,8192]{1,0:T(8,128)(2,1)} %param.34, bf16[512,512]{1,0:T(8,128)(2,1)S(1)} %copy-done.2, f32[512]{0:T(512)S(1)} %copy-done.16, f32[512]{0:T(512)S(1)} %add_rsqrt_fusion.1), kind=kOutput, calls=%fused_computation.5 | convolution fusion | flops 4300210176 | bytes 17305600 | tf_op jit(solution)/shard_map/dot_general | solution.py:184
  220.1 4.3 all-to-all-start
  224.5 6.3 %all-to-all-done = bf16[8,2,5120]{2,1,0:T(2,128)(2,1)S(1)} async-done(((bf16[8,2,5120]{2,1,0:T(2,128)(2,1)}), bf16[8,2,5120]{2,1,0:T(2,128)(2,1)S(1)}, u32[]{:S(2)}, u32[]{:S(2)}) %all-to-all-start) | async-done | bytes 163872 | tf_op jit(solution)/shard_map/all_to_all | solution.py:193
  231.3 5.6 %convolution_convert_fusion.3 = bf16[512,8192]{1,0:T(8,128)(2,1)} fusion(bf16[512,80]{1,0:T(8,128)(2,1)S(1)} %reshape.194, bf16[80,8192]{1,0:T(8,128)(2,1)S(1)} %copy-done), kind=kOutput, calls=%fused_computation.4 | convolution fusion | flops 675282944 | bytes 9781248 | tf_op jit(solution)/shard_map/dot_general | solution.py:79
  236.9 11.6 %copy.53 = bf16[64,8,16,512]{3,2,1,0:T(8,128)(2,1)} copy(bf16[64,8,16,512]{3,1,2,0:T(8,128)(2,1)} %bitcast.115) | data formatting | bytes 16777216
  248.4 5.6 %convolution_convert_fusion.2 = bf16[512,8192]{1,0:T(8,128)(2,1)} fusion(bf16[512,80]{1,0:T(8,128)(2,1)S(1)} %reshape.194, bf16[80,8192]{1,0:T(8,128)(2,1)S(1)} %copy-done.3), kind=kOutput, calls=%fused_computation.3 | convolution fusion | flops 675282944 | bytes 9781248 | tf_op jit(solution)/shard_map/dot_general | solution.py:82
  254.0 11.4 %copy.54 = bf16[64,8,16,512]{3,2,1,0:T(8,128)(2,1)} copy(bf16[64,8,16,512]{3,1,2,0:T(8,128)(2,1)} %bitcast.114) | data formatting | bytes 16777216
  265.3 8.4 %pad_maximum_fusion = bf16[16,1024,512]{1,0,2:T(8,128)(2,1)S(1)} fusion(bf16[16,512,512]{1,0,2:T(8,128)(2,1)} %bitcast.117, bf16[16,512,512]{1,0,2:T(8,128)(2,1)} %bitcast.116), kind=kLoop, calls=%fused_computation | loop fusion | flops 33554432 | bytes 33554432 | tf_op jit(solution)/shard_map/concatenate | solution.py:87
  273.7 12.0 %copy.55 = bf16[64,8,16,1024]{3,1,2,0:T(8,128)(2,1)} copy(bf16[64,8,16,1024]{3,2,1,0:T(8,128)(2,1)S(1)} %bitcast.113) | data formatting | bytes 33554432
  286.5 13.1 %reduce-scatter.9.cloned.1.call-done = bf16[512,512]{0,1:T(8,128)(2,1)} async-done(((bf16[8192,512]{0,1:T(8,128)(2,1)}), bf16[512,512]{0,1:T(8,128)(2,1)}) %reduce-scatter.9.cloned.1.call-update) | async-done | bytes 524304 | tf_op jit(solution)/shard_map/reduce_scatter | solution.py:183
  300.8 112.5 %reduce-scatter.7.cloned.1.call-done = bf16[1024,512]{0,1:T(8,128)(2,1)} async-done(((bf16[16384,512]{0,1:T(8,128)(2,1)}), bf16[1024,512]{0,1:T(8,128)(2,1)}) %reduce-scatter.7.cloned.1.call-update) | async-done | bytes 1048592 | tf_op jit(solution)/shard_map/reduce_scatter | solution.py:197
  418.2 6.9 %fusion.1 = bf16[8192,512]{0,1:T(8,128)(2,1)} fusion(bf16[512,512]{1,0:T(8,128)(2,1)S(1)} %bitcast.122, bf16[512,8192]{1,0:T(8,128)(2,1)S(1)} %bitcast.119), kind=kOutput, calls=%fused_computation.6 | convolution fusion | flops 4299161600 | bytes 17301504 | tf_op jit(solution)/shard_map/dot_general | solution.py:223
  426.0 84.6 %reduce-scatter.11.cloned.1.call-done = bf16[512,512]{0,1:T(8,128)(2,1)} async-done(((bf16[8192,512]{0,1:T(8,128)(2,1)}), bf16[512,512]{0,1:T(8,128)(2,1)}) %reduce-scatter.11.cloned.1.call-update) | async-done | bytes 524304 | tf_op jit(solution)/shard_map/reduce_scatter | solution.py:222
  510.6 2.2 convert_add_fusion
  (146 shorter events, 29.1 us)
Async XLA Ops:
  6.5 224.8 %copy-start = (bf16[80,8192]{1,0:T(8,128)(2,1)S(1)}, bf16[80,8192]{1,0:T(8,128)(2,1)}, u32[]{:S(2)}) copy-start(bf16[80,8192]{1,0:T(8,128)(2,1)} %param.35) | copy-start | bytes 3932164
  6.5 78.3 %copy-start.4 = (bf16[4,256,80]{1,2,0:T(8,128)(2,1)S(1)}, bf16[4,256,80]{1,2,0:T(8,128)(2,1)}, u32[]{:S(2)}) copy-start(bf16[4,256,80]{1,2,0:T(8,128)(2,1)} %param.25) | copy-start | bytes 491524
  6.5 160.1 %reduce-scatter.13.cloned.1.call-start = ((), (), s32[]{:S(2)}) async-start(), calls=%async_computation.8 | async-start | bytes 696320
  6.5 10.8 %collective-permute-start = (bf16[4,256,80]{1,2,0:T(8,128)(2,1)}, bf16[4,256,80]{1,2,0:T(8,128)(2,1)S(1)}, u32[]{:S(2)}, u32[]{:S(2)}) collective-permute-start(bf16[4,256,80]{1,2,0:T(8,128)(2,1)} %param.25), channel_id=1, source_target_pairs={{0,1},{1,2},{2,3},{3,4},{4,5},{5,6},{6,7},{7,8},{8,9},{9,10},{10,1... | collective-permute-start | bytes 491528 | tf_op jit(solution)/shard_map/ppermute | solution.py:20
  17.3 8.7 %collective-permute-start.1 = (bf16[4,256,80]{1,2,0:T(8,128)(2,1)S(1)}, bf16[4,256,80]{1,2,0:T(8,128)(2,1)S(1)}, u32[]{:S(2)}, u32[]{:S(2)}) collective-permute-start(bf16[4,256,80]{1,2,0:T(8,128)(2,1)S(1)} %collective-permute-done), channel_id=1, source_target_pairs={{0,1},{1,2},{2,3},{3,4},{4,5},{5,6},{6,7},{7,8},{8,9},{9,10},{10,1... | collective-permute-start | bytes 491528 | tf_op jit(solution)/shard_map/ppermute | solution.py:20
  17.3 8.7 %collective-permute-start.8 = (bf16[4,256,80]{1,2,0:T(8,128)(2,1)}, bf16[4,256,80]{1,2,0:T(8,128)(2,1)S(1)}, u32[]{:S(2)}, u32[]{:S(2)}) collective-permute-start(bf16[4,256,80]{1,2,0:T(8,128)(2,1)} %param.25), channel_id=1, source_target_pairs={{0,15},{1,0},{2,1},{3,2},{4,3},{5,4},{6,5},{7,6},{8,7},{9,8},{10,9... | collective-permute-start | bytes 491528 | tf_op jit(solution)/shard_map/ppermute | solution.py:22
  26.0 8.6 %collective-permute-start.2 = (bf16[4,256,80]{1,2,0:T(8,128)(2,1)S(1)}, bf16[4,256,80]{1,2,0:T(8,128)(2,1)S(1)}, u32[]{:S(2)}, u32[]{:S(2)}) collective-permute-start(bf16[4,256,80]{1,2,0:T(8,128)(2,1)S(1)} %collective-permute-done.1), channel_id=1, source_target_pairs={{0,1},{1,2},{2,3},{3,4},{4,5},{5,6},{6,7},{7,8},{8,9},{9,10},{10,1... | collective-permute-start | bytes 491528 | tf_op jit(solution)/shard_map/ppermute | solution.py:20
  26.0 8.6 %collective-permute-start.9 = (bf16[4,256,80]{1,2,0:T(8,128)(2,1)S(1)}, bf16[4,256,80]{1,2,0:T(8,128)(2,1)S(1)}, u32[]{:S(2)}, u32[]{:S(2)}) collective-permute-start(bf16[4,256,80]{1,2,0:T(8,128)(2,1)S(1)} %collective-permute-done.8), channel_id=1, source_target_pairs={{0,15},{1,0},{2,1},{3,2},{4,3},{5,4},{6,5},{7,6},{8,7},{9,8},{10,9... | collective-permute-start | bytes 491528 | tf_op jit(solution)/shard_map/ppermute | solution.py:22
  34.6 8.6 %collective-permute-start.3 = (bf16[4,256,80]{1,2,0:T(8,128)(2,1)S(1)}, bf16[4,256,80]{1,2,0:T(8,128)(2,1)S(1)}, u32[]{:S(2)}, u32[]{:S(2)}) collective-permute-start(bf16[4,256,80]{1,2,0:T(8,128)(2,1)S(1)} %collective-permute-done.2), channel_id=1, source_target_pairs={{0,1},{1,2},{2,3},{3,4},{4,5},{5,6},{6,7},{7,8},{8,9},{9,10},{10,1... | collective-permute-start | bytes 491528 | tf_op jit(solution)/shard_map/ppermute | solution.py:20
  34.7 9.7 %collective-permute-start.10 = (bf16[4,256,80]{1,2,0:T(8,128)(2,1)S(1)}, bf16[4,256,80]{1,2,0:T(8,128)(2,1)S(1)}, u32[]{:S(2)}, u32[]{:S(2)}) collective-permute-start(bf16[4,256,80]{1,2,0:T(8,128)(2,1)S(1)} %collective-permute-done.9), channel_id=1, source_target_pairs={{0,15},{1,0},{2,1},{3,2},{4,3},{5,4},{6,5},{7,6},{8,7},{9,8},{10,9... | collective-permute-start | bytes 491528 | tf_op jit(solution)/shard_map/ppermute | solution.py:22
  43.3 8.6 %collective-permute-start.4 = (bf16[4,256,80]{1,2,0:T(8,128)(2,1)S(1)}, bf16[4,256,80]{1,2,0:T(8,128)(2,1)S(1)}, u32[]{:S(2)}, u32[]{:S(2)}) collective-permute-start(bf16[4,256,80]{1,2,0:T(8,128)(2,1)S(1)} %collective-permute-done.3), channel_id=1, source_target_pairs={{0,1},{1,2},{2,3},{3,4},{4,5},{5,6},{6,7},{7,8},{8,9},{9,10},{10,1... | collective-permute-start | bytes 491528 | tf_op jit(solution)/shard_map/ppermute | solution.py:20
  44.4 8.2 %collective-permute-start.11 = (bf16[4,256,80]{1,2,0:T(8,128)(2,1)S(1)}, bf16[4,256,80]{1,2,0:T(8,128)(2,1)S(1)}, u32[]{:S(2)}, u32[]{:S(2)}) collective-permute-start(bf16[4,256,80]{1,2,0:T(8,128)(2,1)S(1)} %collective-permute-done.10), channel_id=1, source_target_pairs={{0,15},{1,0},{2,1},{3,2},{4,3},{5,4},{6,5},{7,6},{8,7},{9,8},{10,9... | collective-permute-start | bytes 491528 | tf_op jit(solution)/shard_map/ppermute | solution.py:22
  51.9 8.9 %collective-permute-start.5 = (bf16[4,256,80]{1,2,0:T(8,128)(2,1)S(1)}, bf16[4,256,80]{1,2,0:T(8,128)(2,1)S(1)}, u32[]{:S(2)}, u32[]{:S(2)}) collective-permute-start(bf16[4,256,80]{1,2,0:T(8,128)(2,1)S(1)} %collective-permute-done.4), channel_id=1, source_target_pairs={{0,1},{1,2},{2,3},{3,4},{4,5},{5,6},{6,7},{7,8},{8,9},{9,10},{10,1... | collective-permute-start | bytes 491528 | tf_op jit(solution)/shard_map/ppermute | solution.py:20
  52.6 9.7 %collective-permute-start.12 = (bf16[4,256,80]{1,2,0:T(8,128)(2,1)S(1)}, bf16[4,256,80]{1,2,0:T(8,128)(2,1)S(1)}, u32[]{:S(2)}, u32[]{:S(2)}) collective-permute-start(bf16[4,256,80]{1,2,0:T(8,128)(2,1)S(1)} %collective-permute-done.11), channel_id=1, source_target_pairs={{0,15},{1,0},{2,1},{3,2},{4,3},{5,4},{6,5},{7,6},{8,7},{9,8},{10,9... | collective-permute-start | bytes 491528 | tf_op jit(solution)/shard_map/ppermute | solution.py:22
  60.8 9.9 %collective-permute-start.6 = (bf16[4,256,80]{1,2,0:T(8,128)(2,1)S(1)}, bf16[4,256,80]{1,2,0:T(8,128)(2,1)}, u32[]{:S(2)}, u32[]{:S(2)}) collective-permute-start(bf16[4,256,80]{1,2,0:T(8,128)(2,1)S(1)} %collective-permute-done.5), channel_id=1, source_target_pairs={{0,1},{1,2},{2,3},{3,4},{4,5},{5,6},{6,7},{7,8},{8,9},{9,10},{10,1... | collective-permute-start | bytes 491528 | tf_op jit(solution)/shard_map/ppermute | solution.py:20
  62.3 9.9 %collective-permute-start.13 = (bf16[4,256,80]{1,2,0:T(8,128)(2,1)S(1)}, bf16[4,256,80]{1,2,0:T(8,128)(2,1)S(1)}, u32[]{:S(2)}, u32[]{:S(2)}) collective-permute-start(bf16[4,256,80]{1,2,0:T(8,128)(2,1)S(1)} %collective-permute-done.12), channel_id=1, source_target_pairs={{0,15},{1,0},{2,1},{3,2},{4,3},{5,4},{6,5},{7,6},{8,7},{9,8},{10,9... | collective-permute-start | bytes 491528 | tf_op jit(solution)/shard_map/ppermute | solution.py:22
  70.7 9.0 %collective-permute-start.7 = (bf16[4,256,80]{1,2,0:T(8,128)(2,1)}, bf16[4,256,80]{1,2,0:T(8,128)(2,1)}, u32[]{:S(2)}, u32[]{:S(2)}) collective-permute-start(bf16[4,256,80]{1,2,0:T(8,128)(2,1)} %collective-permute-done.6), channel_id=1, source_target_pairs={{0,1},{1,2},{2,3},{3,4},{4,5},{5,6},{6,7},{7,8},{8,9},{9,10},{10,1... | collective-permute-start | bytes 491528 | tf_op jit(solution)/shard_map/ppermute | solution.py:20
  72.1 10.6 %collective-permute-start.14 = (bf16[4,256,80]{1,2,0:T(8,128)(2,1)S(1)}, bf16[4,256,80]{1,2,0:T(8,128)(2,1)S(1)}, u32[]{:S(2)}, u32[]{:S(2)}) collective-permute-start(bf16[4,256,80]{1,2,0:T(8,128)(2,1)S(1)} %collective-permute-done.13), channel_id=1, source_target_pairs={{0,15},{1,0},{2,1},{3,2},{4,3},{5,4},{6,5},{7,6},{8,7},{9,8},{10,9... | collective-permute-start | bytes 491528 | tf_op jit(solution)/shard_map/ppermute | solution.py:22
  81.6 4.4 copy-start.11
  81.7 4.4 copy-start.14
  86.1 3.6 copy-start.6
  86.1 3.6 copy-start.13
  86.1 3.6 copy-start.15
  87.5 4.1 copy-start.5
  87.6 5.6 %copy-start.2 = (bf16[512,512]{1,0:T(8,128)(2,1)S(1)}, bf16[512,512]{1,0:T(8,128)(2,1)}, u32[]{:S(2)}) copy-start(bf16[512,512]{1,0:T(8,128)(2,1)} %param.19) | copy-start | bytes 1572868
  87.6 119.3 %copy-start.16 = (f32[512]{0:T(512)S(1)}, f32[512]{0:T(512)}, u32[]{:S(2)}) copy-start(f32[512]{0:T(512)} %param.20) | copy-start | bytes 6148
  93.1 206.5 %reduce-scatter.9.cloned.1.call-start = ((), (), s32[]{:S(2)}) async-start(), calls=%async_computation.6 | async-start | bytes 8912896 | tf_op jit(solution)/shard_map/reduce_scatter | solution.py:183
  220.1 10.8 %all-to-all-start = ((bf16[8,2,5120]{2,1,0:T(2,128)(2,1)}), bf16[8,2,5120]{2,1,0:T(2,128)(2,1)S(1)}, u32[]{:S(2)}, u32[]{:S(2)}) async-start(bf16[8,2,5120]{2,1,0:T(2,128)(2,1)} %copy.39), calls=%async_computation | async-start | bytes 327680 | tf_op jit(solution)/shard_map/all_to_all | solution.py:193
  224.4 188.9 %reduce-scatter.7.cloned.1.call-start = ((), (), s32[]{:S(2)}) async-start(), calls=%async_computation.5 | async-start | bytes 17825792 | tf_op jit(solution)/shard_map/reduce_scatter | solution.py:197
  236.9 11.6 %copy-start.3 = (bf16[80,8192]{1,0:T(8,128)(2,1)S(1)}, bf16[80,8192]{1,0:T(8,128)(2,1)}, u32[]{:S(2)}) copy-start(bf16[80,8192]{1,0:T(8,128)(2,1)} %param.36) | copy-start | bytes 3932164
  285.8 224.8 %reduce-scatter.11.cloned.1.call-start = ((), (), s32[]{:S(2)}) async-start(), calls=%async_computation.7 | async-start | bytes 8912896 | tf_op jit(solution)/shard_map/reduce_scatter | solution.py:222
  425.2 87.6 %copy-start.1 = (bf16[80,8192]{1,0:T(8,128)(2,1)S(1)}, bf16[80,8192]{1,0:T(8,128)(2,1)}, u32[]{:S(2)}) copy-start(bf16[80,8192]{1,0:T(8,128)(2,1)} %param.35) | copy-start | bytes 3932164
  (7 other events, 10.5 us)
Sparse Core Ops, SparseCore 0:
  93.2 73.3 reduce-scatter.12
  217.2 82.2 reduce-scatter.8
  302.9 110.2 reduce-scatter.6
  425.3 85.1 reduce-scatter.10
